TPU v7x, 32 devices: a whole 2x2x4 slice. The times are simulated.
32 devices in a mesh: dp: 8 (over z, x), group: 4 (over y, core).
Axes of the slice: x: 2, y: 2, z: 4, core: 2. Of those that a mesh axis runs over, the one named last changes fastest.
Arguments:
- partials: float32 [4, 54, 1024, 1024], P('group', None, 'dp'), may hold values from -0.3 to 0.3
- second_moment: float32 [54, 1024, 1024], P(None, 'dp', 'group'), may hold values from 0.0001 to 0.01
- left_stats: float32 [54, 1024, 1024], P(None, 'dp', 'group'), may hold values from -3 to 3
- right_stats: float32 [54, 1024, 1024], P(None, 'dp', 'group'), may hold values from -3 to 3
- left_roots: bfloat16 [54, 1024, 1024], P(None, 'dp', 'group'), may hold values from -0.2 to 2.1
- right_roots: bfloat16 [54, 1024, 1024], P(None, 'dp', 'group'), may hold values from -0.2 to 2.1
- norm_partials: float32 [8, 4, 2, 2048], P('dp', 'group'), may hold values from -0.012 to 0.012
- norm_moment: float32 [2, 2048], replicated, may hold values from 0.0001 to 0.01
Outputs:
- block_step: bfloat16 [54, 1024, 1024], P(None, 'dp', 'group')
- new_moment: float32 [54, 1024, 1024], P(None, 'dp', 'group')
- new_left: float32 [54, 1024, 1024], P(None, 'dp', 'group')
- new_right: float32 [54, 1024, 1024], P(None, 'dp', 'group')
- norm_step: float32 [2, 2048], replicated
- new_norm_moment: float32 [2, 2048], replicated
All inputs are finite; a program needn't handle non-finite values.
Results may differ from a plain program's by a relative error of at most 0.0042.
The roundings to bfloat16 on the way count: a program that leaves them out, or rounds other values in their place, can miss the bound.
Values may be sent and summed in bfloat16 or wider, within the bound.
No kernel may reach another device: no remote copies, remote signals or barrier semaphores. Data moves between devices by JAX's collectives and lax.ppermute only.
A program may use at most 384 MiB of HBM per device.

v0:
```python
import jax
import jax.numpy as jnp
from jax import lax
from jax.sharding import PartitionSpec as P

EPS_ADAM = 1e-08
EPS_GRAFT = 1e-06


def on_device(
    partials,
    second_moment,
    left_stats,
    right_stats,
    left_roots,
    right_roots,
    norm_partials,
    norm_moment,
):
    n_dp = lax.axis_size("dp")
    me_dp = lax.axis_index("dp")
    me_group = lax.axis_index("group")
    count = second_moment.shape[0]
    rows = partials.shape[2]
    quarter = second_moment.shape[2]
    width = rows * n_dp
    cap = -(-count // n_dp)
    slots = cap * n_dp
    lower = me_group * quarter

    def to_owners(blocks):
        padded = jnp.pad(blocks, ((0, slots - count), (0, 0), (0, 0)))
        sent = lax.all_to_all(padded.reshape(n_dp, cap, rows, quarter), "dp", 0, 0, tiled=True)
        return sent.transpose(1, 0, 2, 3).reshape(cap, width, quarter)

    def to_keepers(owned):
        back = lax.all_to_all(owned, "dp", 0, 0, tiled=True)
        return back.reshape(slots, rows, quarter)[:count]

    left_root = to_owners(left_roots)
    right_root = to_owners(right_roots)
    local_norm = norm_partials[0, 0]
    norm_grad = jnp.sum(lax.all_gather(local_norm, ("dp", "group")), axis=0)
    grad = lax.psum_scatter(partials[0], "group", scatter_dimension=2, tiled=True)
    grad, left_root, right_root = lax.optimization_barrier((grad, left_root, right_root))
    new_moment = 0.99 * second_moment + 0.01 * grad * grad
    adam = grad / (jnp.sqrt(new_moment) + EPS_ADAM)
    adam_part = jnp.sum(adam * adam, axis=(1, 2))
    adam_sq = jnp.sum(lax.all_gather(adam_part, ("dp", "group")), axis=0)
    grad_low = grad.astype(jnp.bfloat16)
    mine = to_owners(grad_low)
    piece = lax.all_gather(mine, "group", axis=2, tiled=True)
    own_rows = lax.dynamic_slice_in_dim(piece, lower, quarter, 1)
    piece4 = piece.reshape(cap, n_dp, rows, width)
    gram_left = jnp.einsum("cdim,cjm->dcij", piece4, own_rows, preferred_element_type=jnp.float32)
    gram_right = jnp.einsum("cim,cij->cmj", piece, mine, preferred_element_type=jnp.float32)
    gram_right = gram_right.reshape(cap, n_dp, rows, quarter).transpose(1, 0, 2, 3)
    left_term = to_keepers(gram_left.astype(jnp.bfloat16)).astype(jnp.float32)
    right_term = to_keepers(gram_right.astype(jnp.bfloat16)).astype(jnp.float32)
    half = jnp.einsum("cim,cmj->cij", piece, right_root, preferred_element_type=jnp.float32)
    half = half.astype(jnp.bfloat16)
    full_left = lax.all_gather(left_root, "group", axis=2, tiled=True)
    full_left4 = full_left.reshape(cap, n_dp, rows, width)
    direction = jnp.einsum("cdim,cmj->dcij", full_left4, half, preferred_element_type=jnp.float32)
    direction_sq = lax.psum(jnp.sum(direction * direction, axis=(0, 2, 3)), "group")
    adam_pad = jnp.pad(adam_sq, (0, slots - count))
    adam_owned = lax.dynamic_slice_in_dim(adam_pad, me_dp * cap, cap)
    ratio = jnp.sqrt(adam_owned / (direction_sq + EPS_GRAFT))
    scaled = (ratio[None, :, None, None] * direction).astype(jnp.bfloat16)
    block_step = to_keepers(scaled)
    new_left = 0.95 * left_stats + 0.05 * left_term
    new_right = 0.95 * right_stats + 0.05 * right_term
    new_norm_moment = 0.99 * norm_moment + 0.01 * norm_grad * norm_grad
    norm_step = norm_grad / (jnp.sqrt(new_norm_moment) + EPS_ADAM)
    return (block_step, new_moment, new_left, new_right, norm_step, new_norm_moment)


def solution(mesh):
    return jax.shard_map(
        on_device,
        mesh=mesh,
        in_specs=(
            P("group", None, "dp", None),
            P(None, "dp", "group"),
            P(None, "dp", "group"),
            P(None, "dp", "group"),
            P(None, "dp", "group"),
            P(None, "dp", "group"),
            P("dp", "group", None, None),
            P(),
        ),
        out_specs=(
            P(None, "dp", "group"),
            P(None, "dp", "group"),
            P(None, "dp", "group"),
            P(None, "dp", "group"),
            P(),
            P(),
        ),
        check_vma=False,
    )
```

profile of v0, /device:TPU:17, one launch (start us, length us, event | category | flops | bytes accessed | tf_op | source)
XLA Modules:
  0.0 766.6 jit_solution(13714949214837697143)
XLA Ops:
  9.2 2.2 pad.14
  11.4 5.8 all-to-all-start
  17.3 2.2 pad.15
  19.5 75.9 %all-to-all-done = bf16[8,7,128,256]{3,2,1,0:T(8,128)(2,1)} async-done(((bf16[8,7,128,256]{3,2,1,0:T(8,128)(2,1)}), bf16[8,7,128,256]{3,2,1,0:T(8,128)(2,1)}, u32[]{:S(2)}, u32[]{:S(2)}) %all-to-all-start) | async-done | bytes 3670048 | tf_op jit(solution)/shard_map/all_to_all | solution.py:33
  95.4 7.8 %all-to-all-start.1 = ((bf16[8,7,128,256]{3,2,1,0:T(8,128)(2,1)}), bf16[8,7,128,256]{3,2,1,0:T(8,128)(2,1)}, u32[]{:S(2)}, u32[]{:S(2)}) async-start(bf16[8,7,128,256]{3,2,1,0:T(8,128)(2,1)} %bitcast.44), calls=%async_computation.2 | async-start | bytes 7340032 | tf_op jit(solution)/shard_map/all_to_all | solution.py:33
  103.1 4.3 copy.42
  107.4 73.2 %all-to-all-done.1 = bf16[8,7,128,256]{3,2,1,0:T(8,128)(2,1)} async-done(((bf16[8,7,128,256]{3,2,1,0:T(8,128)(2,1)}), bf16[8,7,128,256]{3,2,1,0:T(8,128)(2,1)}, u32[]{:S(2)}, u32[]{:S(2)}) %all-to-all-start.1) | async-done | bytes 3670048 | tf_op jit(solution)/shard_map/all_to_all | solution.py:33
  180.7 4.3 copy.43
  184.9 27.7 %reduce-scatter.2.cloned.1.call-done = f32[54,128,256]{2,1,0:T(8,128)} async-done(((f32[54,128,1024]{2,1,0:T(8,128)}), f32[54,128,256]{2,1,0:T(8,128)}) %reduce-scatter.2.cloned.1.call-update) | async-done | bytes 7077904 | tf_op jit(solution)/shard_map/reduce_scatter | solution.py:44
  212.7 11.8 %multiply_reduce_fusion.1 = (f32[54]{0:T(128)S(1)}, f32[54,128,256]{2,1,0:T(8,128)}, bf16[54,128,256]{2,1,0:T(8,128)(2,1)S(1)}) fusion(f32[54,128,256]{2,1,0:T(8,128)} %reduce-scatter.2.cloned.1.call-done, f32[54,128,256]{2,1,0:T(8,128)} %param.9), kind=kLoop, calls=%fused_computation.6 | loop fusion | flops 15925194 | bytes 24772824 | tf_op jit(solution)/shard_map/reduce_sum | solution.py:48
  225.0 85.1 %all_to_all.30 = bf16[8,7,128,256]{3,2,1,0:T(8,128)(2,1)S(1)} all-to-all(bf16[8,7,128,256]{3,2,1,0:T(8,128)(2,1)S(1)} %bitcast.46), channel_id=1, replica_groups=mesh['dp'=8,'group'=4] {'dp'}, dimensions={0} | all-to-all | bytes 7340032 | tf_op jit(solution)/shard_map/all_to_all | solution.py:33
  310.1 2.3 copy.44
  312.7 40.1 %all-reduce.4 = f32[1728]{0:T(1024)S(1)} all-reduce(f32[1728]{0:T(1024)S(1)} %dynamic-update-slice), channel_id=2, replica_groups=mesh['dp'=8,'group'=4] {'dp','group'}, use_global_device_ids=true, to_apply=%add.4 | all-reduce | flops 1728 | bytes 13824
  353.0 57.4 %all-gather.5.cloned.1.call-done = bf16[7,1024,1024]{2,1,0:T(8,128)(2,1)} async-done(((bf16[7,1024,256]{2,1,0:T(8,128)(2,1)}), bf16[7,1024,1024]{2,1,0:T(8,128)(2,1)}) %all-gather.5.cloned.1.call-update) | async-done | bytes 14680080 | tf_op jit(solution)/shard_map/all_gather | solution.py:52
  410.4 17.6 %multiply_reduce_fusion = (f32[7]{0:T(128)S(1)}, f32[7,256,8,128]{3,1,2,0:T(8,128)}) fusion(bf16[7,8,128,1024]{3,2,1,0:T(8,128)(2,1)} %bitcast.57, bf16[7,1024,1024]{2,1,0:T(8,128)(2,1)} %all-gather.5.cloned.1.call-done, bf16[7,1024,256]{2,1,0:T(8,128)(2,1)} %bitcast.54), kind=kOutput, calls=%fused_computation.2 | convolution fusion | flops 7521697792 | bytes 40370204 | tf_op jit(solution)/shard_map/cdim,cmj->dcij/dot_general | solution.py:64
  427.9 5.2 psum.7
  433.3 4.1 fusion.1
  437.4 2.3 copy.46
  439.6 5.4 all-to-all-start.3
  445.0 8.5 %convert_bitcast_fusion = bf16[8,7,128,256]{2,3,0,1:T(8,128)(2,1)S(1)} fusion(bf16[7,8,128,1024]{3,2,1,0:T(8,128)(2,1)} %bitcast.56, bf16[7,1024,1024]{2,1,0:T(8,128)(2,1)} %all-gather.5.cloned.1.call-done, s32[]{:T(128)S(6)} %select_n.7), kind=kOutput, calls=%fused_computation.13 | convolution fusion | flops 3759931392 | bytes 22020100 | tf_op jit(solution)/shard_map/cdim,cjm->dcij/dot_general | solution.py:55
  453.5 2.1 copy.48
  455.6 67.1 %all-to-all-done.3 = bf16[8,7,128,256]{2,3,1,0:T(8,128)(2,1)} async-done(((bf16[8,7,128,256]{2,3,1,0:T(8,128)(2,1)}), bf16[8,7,128,256]{2,3,1,0:T(8,128)(2,1)}, u32[]{:S(2)}, u32[]{:S(2)}) %all-to-all-start.3) | async-done | bytes 3670048 | tf_op jit(solution)/shard_map/all_to_all | solution.py:37
  522.8 8.1 %all-to-all-start.4 = ((bf16[8,7,128,256]{2,3,1,0:T(8,128)(2,1)}), bf16[8,7,128,256]{2,3,1,0:T(8,128)(2,1)}, u32[]{:S(2)}, u32[]{:S(2)}) async-start(bf16[8,7,128,256]{2,3,1,0:T(8,128)(2,1)} %copy.48), calls=%async_computation.5 | async-start | bytes 7340032 | tf_op jit(solution)/shard_map/all_to_all | solution.py:37
  530.9 9.0 %convolution_convert_fusion = bf16[7,1024,256]{2,1,0:T(8,128)(2,1)S(1)} fusion(bf16[7,1024,1024]{2,1,0:T(8,128)(2,1)} %all-gather.5.cloned.1.call-done, bf16[7,1024,256]{2,1,0:T(8,128)(2,1)} %bitcast.48), kind=kOutput, calls=%fused_computation.17 | convolution fusion | flops 3759931392 | bytes 22020096 | tf_op jit(solution)/shard_map/cim,cij->cmj/dot_general | solution.py:56
  542.0 66.3 %all-to-all-done.4 = bf16[8,7,128,256]{2,3,1,0:T(8,128)(2,1)} async-done(((bf16[8,7,128,256]{2,3,1,0:T(8,128)(2,1)}), bf16[8,7,128,256]{2,3,1,0:T(8,128)(2,1)}, u32[]{:S(2)}, u32[]{:S(2)}) %all-to-all-start.4) | async-done | bytes 3670048 | tf_op jit(solution)/shard_map/all_to_all | solution.py:37
  608.2 8.5 %all-to-all-start.5 = ((bf16[8,7,128,256]{3,2,1,0:T(8,128)(2,1)}), bf16[8,7,128,256]{3,2,1,0:T(8,128)(2,1)}, u32[]{:S(2)}, u32[]{:S(2)}) async-start(bf16[8,7,128,256]{3,2,1,0:T(8,128)(2,1)} %bitcast.50), calls=%async_computation.6 | async-start | bytes 7340032 | tf_op jit(solution)/shard_map/all_to_all | solution.py:37
  616.8 108.7 %all-gather.1 = f32[32,1,2,2048]{3,2,1,0:T(2,128)S(1)} all-gather(f32[1,1,2,2048]{3,2,1,0:T(2,128)S(1)} %copy-done.2), channel_id=3, replica_groups=mesh['dp'=8,'group'=4] {'dp','group'}, dimensions={0}, use_global_device_ids=true | all-gather | bytes 540672 | tf_op jit(solution)/shard_map/all_gather | solution.py:43
  726.2 6.2 copy.47
  732.4 4.2 slice.12
  736.6 6.2 copy.49
  742.8 8.6 %multiply_add_fusion.1 = f32[54,128,256]{2,1,0:T(8,128)} fusion(f32[54,128,256]{2,1,0:T(8,128)} %param.10, bf16[56,128,256]{2,1,0:T(8,128)(2,1)} %bitcast.53), kind=kLoop, calls=%fused_computation.5 | loop fusion | flops 7077888 | bytes 17694720 | tf_op jit(solution)/shard_map/add | solution.py:71
  751.5 8.6 %multiply_add_fusion = f32[54,128,256]{2,1,0:T(8,128)} fusion(f32[54,128,256]{2,1,0:T(8,128)} %param.11, bf16[56,128,256]{2,1,0:T(8,128)(2,1)} %bitcast.21), kind=kLoop, calls=%fused_computation.4 | loop fusion | flops 7077888 | bytes 17694720 | tf_op jit(solution)/shard_map/add | solution.py:72
  (25 shorter events, 6.0 us)
Async XLA Ops:
  7.2 205.5 %reduce-scatter.2.cloned.1.call-start = ((), (), s32[]{:S(2)}) async-start(), calls=%async_computation.7 | async-start | bytes 35389440 | tf_op jit(solution)/shard_map/reduce_scatter | solution.py:44
  7.2 2.0 copy-start
  11.4 5.8 copy-start.1
  11.4 83.9 %all-to-all-start = ((bf16[8,7,128,256]{3,2,1,0:T(8,128)(2,1)}), bf16[8,7,128,256]{3,2,1,0:T(8,128)(2,1)}, u32[]{:S(2)}, u32[]{:S(2)}) async-start(bf16[8,7,128,256]{3,2,1,0:T(8,128)(2,1)} %bitcast.45), calls=%async_computation.1 | async-start | bytes 7340032 | tf_op jit(solution)/shard_map/all_to_all | solution.py:33
  95.4 85.3 %all-to-all-start.1 = ((bf16[8,7,128,256]{3,2,1,0:T(8,128)(2,1)}), bf16[8,7,128,256]{3,2,1,0:T(8,128)(2,1)}, u32[]{:S(2)}, u32[]{:S(2)}) async-start(bf16[8,7,128,256]{3,2,1,0:T(8,128)(2,1)} %bitcast.44), calls=%async_computation.2 | async-start | bytes 7340032 | tf_op jit(solution)/shard_map/all_to_all | solution.py:33
  103.1 249.8 %all-gather.7.cloned.1.call-start = ((), (), s32[]{:S(2)}) async-start(), calls=%async_computation.9 | async-start | bytes 18350080 | tf_op jit(solution)/shard_map/all_gather | solution.py:62
  212.7 197.7 %all-gather.5.cloned.1.call-start = ((), (), s32[]{:S(2)}) async-start(), calls=%async_computation.8 | async-start | bytes 18350080 | tf_op jit(solution)/shard_map/all_gather | solution.py:52
  439.6 83.1 %all-to-all-start.3 = ((bf16[8,7,128,256]{2,3,1,0:T(8,128)(2,1)}), bf16[8,7,128,256]{2,3,1,0:T(8,128)(2,1)}, u32[]{:S(2)}, u32[]{:S(2)}) async-start(bf16[8,7,128,256]{2,3,1,0:T(8,128)(2,1)} %copy.46), calls=%async_computation.4 | async-start | bytes 7340032 | tf_op jit(solution)/shard_map/all_to_all | solution.py:37
  522.8 85.5 %all-to-all-start.4 = ((bf16[8,7,128,256]{2,3,1,0:T(8,128)(2,1)}), bf16[8,7,128,256]{2,3,1,0:T(8,128)(2,1)}, u32[]{:S(2)}, u32[]{:S(2)}) async-start(bf16[8,7,128,256]{2,3,1,0:T(8,128)(2,1)} %copy.48), calls=%async_computation.5 | async-start | bytes 7340032 | tf_op jit(solution)/shard_map/all_to_all | solution.py:37
  539.9 76.9 %copy-start.2 = (f32[1,1,2,2048]{3,2,1,0:T(2,128)S(1)}, f32[1,1,2,2048]{3,2,1,0:T(2,128)}, u32[]{:S(2)}) copy-start(f32[1,1,2,2048]{3,2,1,0:T(2,128)} %param.14) | copy-start | bytes 49156
  539.9 185.7 %copy-start.3 = (f32[2,2048]{1,0:T(2,128)S(1)}, f32[2,2048]{1,0:T(2,128)}, u32[]{:S(2)}) copy-start(f32[2,2048]{1,0:T(2,128)} %param.15) | copy-start | bytes 49156
  608.2 143.2 %all-to-all-start.5 = ((bf16[8,7,128,256]{3,2,1,0:T(8,128)(2,1)}), bf16[8,7,128,256]{3,2,1,0:T(8,128)(2,1)}, u32[]{:S(2)}, u32[]{:S(2)}) async-start(bf16[8,7,128,256]{3,2,1,0:T(8,128)(2,1)} %bitcast.50), calls=%async_computation.6 | async-start | bytes 7340032 | tf_op jit(solution)/shard_map/all_to_all | solution.py:37
Sparse Core Ops, SparseCore 0:
  10.6 201.9 reduce-scatter.1
  214.8 96.3 all-gather.6
  313.5 96.8 all-gather.4
where the time goes:
time: 768 us; the launch traced here: 767 us
  waiting for transfers between devices  368 us (48%)
  blocking collectives  239 us (31%)
  local copies, waits for them, and re-layouts  40.5 us (5%)
  starting transfers between devices  35.8 us (5%)
  matrix products  35 us (5%)
  other arithmetic  34 us (4%)
  between operations  13.8 us (2%)
    all_to_all x2, waiting for transfers between devices, to_owners(): lax.all_to_all(padded.reshape(n_dp, cap, rows, quarter), 'dp', 0, 0, tile...  149 us
    all_to_all x3, waiting for transfers between devices, to_keepers(): back = lax.all_to_all(owned, 'dp', 0, 0, tiled=True)  133 us
    all_gather x1, blocking collectives, on_device(): norm_grad = jnp.sum(lax.all_gather(local_norm, ('dp', 'group')), axis=0)  109 us
    all_to_all x1, blocking collectives, to_owners(): lax.all_to_all(padded.reshape(n_dp, cap, rows, quarter), 'dp', 0, 0, tile...  85.1 us
    all_gather x1, waiting for transfers between devices, on_device(): piece = lax.all_gather(mine, 'group', axis=2, tiled=True)  57.4 us
    unnamed x1, blocking collectives  40.1 us
    reduce_scatter x1, waiting for transfers between devices, on_device(): lax.psum_scatter(partials[0], 'group', scatter_dimension=2, tiled=True)  27.7 us
    all_to_all x3, starting transfers between devices, to_keepers(): back = lax.all_to_all(owned, 'dp', 0, 0, tiled=True)  22.1 us
  transfers between devices with their start and end apart: 8, of which 6 were waited for; matrix products, arithmetic and copies ran while one was open for 10% of the time, Pallas kernels for 0%

commit v1 on v0

--- a/solution.py
+++ b/solution.py
@@ -49,7 +49,13 @@
     adam_sq = jnp.sum(lax.all_gather(adam_part, ("dp", "group")), axis=0)
     grad_low = grad.astype(jnp.bfloat16)
     mine = to_owners(grad_low)
-    piece = lax.all_gather(mine, "group", axis=2, tiled=True)
+    size = lax.axis_size("group")
+    held, pieces = (mine, [mine])
+    for _ in range(size - 1):
+        held = lax.ppermute(held, "group", [(i, (i + 1) % size) for i in range(size)])
+        pieces.insert(0, held)
+    line = jnp.concatenate(pieces, axis=2)
+    piece = jnp.roll(line, (lax.axis_index("group") + 1) * mine.shape[2], axis=2)
     own_rows = lax.dynamic_slice_in_dim(piece, lower, quarter, 1)
     piece4 = piece.reshape(cap, n_dp, rows, width)
     gram_left = jnp.einsum("cdim,cjm->dcij", piece4, own_rows, preferred_element_type=jnp.float32)

time: 768 us -> 939 us (1.22)
  waiting for transfers between devices: 368 us -> 438 us
  blocking collectives: 239 us -> 300 us
  local copies, waits for them, and re-layouts: 40.5 us -> 77 us
    ppermute x0 -> x3, waiting for transfers between devices: none -> 196 us  [on_device(): lax.ppermute(held, 'group', [(i, (i + 1) % size) for i in range(size)])]
    all_to_all x3, waiting for transfers between devices: 133 us -> 65.2 us  [to_keepers(): back = lax.all_to_all(owned, 'dp', 0, 0, tiled=True)]
    unnamed x1, blocking collectives: 40.1 us -> 99.6 us
    all_gather x1 -> x0, waiting for transfers between devices: 57.4 us -> none  [on_device(): piece = lax.all_gather(mine, 'group', axis=2, tiled=True)]
    unnamed x10 -> x25, local copies, waits for them, and re-layouts: 1.61 us -> 29.1 us
  transfers between devices with their start and end apart: 8 -> 10, of which waited for: 6 -> 7; matrix products, arithmetic and copies ran while one was open for 10% -> 11% of each run, Pallas kernels for 0% -> 0%
where the time goes in v1:
time: 939 us; the launch traced here: 938 us
  waiting for transfers between devices  438 us (47%)
  blocking collectives  300 us (32%)
  local copies, waits for them, and re-layouts  77 us (8%)
  starting transfers between devices  41.5 us (4%)
  matrix products  36.2 us (4%)
  other arithmetic  29.8 us (3%)
  between operations  14.2 us (2%)
    ppermute x3, waiting for transfers between devices, on_device(): lax.ppermute(held, 'group', [(i, (i + 1) % size) for i in range(size)])  196 us
    all_to_all x2, waiting for transfers between devices, to_owners(): lax.all_to_all(padded.reshape(n_dp, cap, rows, quarter), 'dp', 0, 0, tile...  149 us
    all_gather x1, blocking collectives, on_device(): norm_grad = jnp.sum(lax.all_gather(local_norm, ('dp', 'group')), axis=0)  109 us
    unnamed x1, blocking collectives  99.6 us
    all_to_all x1, blocking collectives, to_owners(): lax.all_to_all(padded.reshape(n_dp, cap, rows, quarter), 'dp', 0, 0, tile...  85.1 us
    all_to_all x3, waiting for transfers between devices, to_keepers(): back = lax.all_to_all(owned, 'dp', 0, 0, tiled=True)  65.2 us
    unnamed x25, local copies, waits for them, and re-layouts  29.1 us
    reduce_scatter x1, waiting for transfers between devices, on_device(): lax.psum_scatter(partials[0], 'group', scatter_dimension=2, tiled=True)  27.8 us
  transfers between devices with their start and end apart: 10, of which 7 were waited for; matrix products, arithmetic and copies ran while one was open for 11% of the time, Pallas kernels for 0%

profile of v1, /device:TPU:17, one launch (start us, length us, event | category | flops | bytes accessed | tf_op | source)
XLA Modules:
  0.0 937.6 jit_solution(4889411410901380477)
XLA Ops:
  11.4 5.8 all-to-all-start
  19.5 75.9 %all-to-all-done = bf16[8,7,128,256]{3,2,1,0:T(8,128)(2,1)} async-done(((bf16[8,7,128,256]{3,2,1,0:T(8,128)(2,1)}), bf16[8,7,128,256]{3,2,1,0:T(8,128)(2,1)}, u32[]{:S(2)}, u32[]{:S(2)}) %all-to-all-start) | async-done | bytes 3670048 | tf_op jit(solution)/shard_map/all_to_all | solution.py:33
  95.4 7.8 all-to-all-start.1
  103.1 4.3 copy.42
  107.4 73.2 %all-to-all-done.1 = bf16[8,7,128,256]{3,2,1,0:T(8,128)(2,1)} async-done(((bf16[8,7,128,256]{3,2,1,0:T(8,128)(2,1)}), bf16[8,7,128,256]{3,2,1,0:T(8,128)(2,1)}, u32[]{:S(2)}, u32[]{:S(2)}) %all-to-all-start.1) | async-done | bytes 3670048 | tf_op jit(solution)/shard_map/all_to_all | solution.py:33
  180.6 4.2 copy.43
  184.9 27.8 %reduce-scatter.2.cloned.1.call-done = f32[54,128,256]{2,1,0:T(8,128)} async-done(((f32[54,128,1024]{2,1,0:T(8,128)}), f32[54,128,256]{2,1,0:T(8,128)}) %reduce-scatter.2.cloned.1.call-update) | async-done | bytes 7077904 | tf_op jit(solution)/shard_map/reduce_scatter | solution.py:44
  212.6 11.6 %multiply_reduce_fusion.1 = (f32[54]{0:T(128)S(1)}, f32[54,128,256]{2,1,0:T(8,128)}, bf16[54,128,256]{2,1,0:T(8,128)(2,1)S(1)}) fusion(f32[54,128,256]{2,1,0:T(8,128)} %reduce-scatter.2.cloned.1.call-done, f32[54,128,256]{2,1,0:T(8,128)} %param.9), kind=kLoop, calls=%fused_computation.6 | loop fusion | flops 15925194 | bytes 24772824 | tf_op jit(solution)/shard_map/reduce_sum | solution.py:48
  224.8 85.1 %all_to_all.30 = bf16[8,7,128,256]{3,2,1,0:T(8,128)(2,1)S(1)} all-to-all(bf16[8,7,128,256]{3,2,1,0:T(8,128)(2,1)S(1)} %bitcast.46), channel_id=1, replica_groups=mesh['dp'=8,'group'=4] {'dp'}, dimensions={0} | all-to-all | bytes 7340032 | tf_op jit(solution)/shard_map/all_to_all | solution.py:33
  313.9 96.8 %collective-permute-done = bf16[7,1024,256]{2,1,0:T(8,128)(2,1)} collective-permute-done((bf16[7,1024,256]{2,1,0:T(8,128)(2,1)}, bf16[7,1024,256]{2,1,0:T(8,128)(2,1)}, u32[]{:S(2)}, u32[]{:S(2)}) %collective-permute-start) | collective-permute-done | bytes 3670048 | tf_op jit(solution)/shard_map/ppermute | solution.py:55
  413.2 58.8 %collective-permute-done.1 = bf16[7,1024,256]{2,1,0:T(8,128)(2,1)} collective-permute-done((bf16[7,1024,256]{2,1,0:T(8,128)(2,1)}, bf16[7,1024,256]{2,1,0:T(8,128)(2,1)}, u32[]{:S(2)}, u32[]{:S(2)}) %collective-permute-start.1) | collective-permute-done | bytes 3670048 | tf_op jit(solution)/shard_map/ppermute | solution.py:55
  474.4 40.1 %collective-permute-done.2 = bf16[7,1024,256]{2,1,0:T(8,128)(2,1)} collective-permute-done((bf16[7,1024,256]{2,1,0:T(8,128)(2,1)}, bf16[7,1024,256]{2,1,0:T(8,128)(2,1)}, u32[]{:S(2)}, u32[]{:S(2)}) %collective-permute-start.2) | collective-permute-done | bytes 3670048 | tf_op jit(solution)/shard_map/ppermute | solution.py:55
  517.1 2.6 constant_dynamic-update-slice_fusion.6
  524.8 2.6 constant_dynamic-update-slice_fusion.3
  535.1 9.7 %copy-done.1 = bf16[7,1024,2048]{2,1,0:T(8,128)(2,1)} copy-done((bf16[7,1024,2048]{2,1,0:T(8,128)(2,1)}, bf16[7,1024,2048]{2,1,0:T(8,128)(2,1)S(1)}, u32[]{:S(2)}) %copy-start.1) | copy-done | bytes 29360152
  544.8 6.2 constant_dynamic-slice_fusion
  551.0 8.9 convolution_convert_fusion
  562.0 6.0 all-to-all-start.5
  568.0 9.6 %convert_bitcast_fusion = bf16[8,7,128,256]{2,3,0,1:T(8,128)(2,1)S(1)} fusion(bf16[7,8,128,1024]{3,2,1,0:T(8,128)(2,1)} %bitcast.50, bf16[7,1024,2048]{2,1,0:T(8,128)(2,1)} %copy-done.1, s32[]{:T(128)S(6)} %select_n.27, s32[]{:T(128)S(6)} %select_n.28), kind=kOutput, calls=%fused_computation.13 | convolution fusion | flops 3759931392 | bytes 22020104 | tf_op jit(solution)/shard_map/cdim,cjm->dcij/dot_general | solution.py:61
  579.7 65.2 %all-to-all-done.5 = bf16[8,7,128,256]{3,2,1,0:T(8,128)(2,1)} async-done(((bf16[8,7,128,256]{3,2,1,0:T(8,128)(2,1)}), bf16[8,7,128,256]{3,2,1,0:T(8,128)(2,1)}, u32[]{:S(2)}, u32[]{:S(2)}) %all-to-all-start.5) | async-done | bytes 3670048 | tf_op jit(solution)/shard_map/all_to_all | solution.py:37
  644.9 9.0 all-to-all-start.4
  654.0 99.6 %all-reduce.4 = f32[1728]{0:T(1024)S(1)} all-reduce(f32[1728]{0:T(1024)S(1)} %dynamic-update-slice), channel_id=2, replica_groups=mesh['dp'=8,'group'=4] {'dp','group'}, use_global_device_ids=true, to_apply=%add.4 | all-reduce | flops 1728 | bytes 13824
  753.8 17.6 %multiply_reduce_fusion = (f32[7]{0:T(128)S(1)}, f32[7,256,8,128]{3,1,2,0:T(8,128)}) fusion(bf16[7,8,128,1024]{3,2,1,0:T(8,128)(2,1)} %bitcast.57, bf16[7,1024,1024]{2,1,0:T(8,128)(2,1)} %constant_dynamic-slice_fusion, bf16[7,1024,256]{2,1,0:T(8,128)(2,1)} %bitcast.55), kind=kOutput, calls=%fused_computation.2 | convolution fusion | flops 7521697792 | bytes 40370204 | tf_op jit(solution)/shard_map/cdim,cmj->dcij/dot_general | solution.py:70
  771.4 7.1 psum.7
  778.6 4.1 fusion.1
  785.0 6.3 all-to-all-start.3
  791.3 108.6 %all-gather.1 = f32[32,1,2,2048]{3,2,1,0:T(2,128)S(1)} all-gather(f32[1,1,2,2048]{3,2,1,0:T(2,128)S(1)} %copy-done.4), channel_id=3, replica_groups=mesh['dp'=8,'group'=4] {'dp','group'}, dimensions={0}, use_global_device_ids=true | all-gather | bytes 540672 | tf_op jit(solution)/shard_map/all_gather | solution.py:43
  900.8 6.3 copy.49
  907.1 8.8 multiply_add_fusion
  915.9 4.4 multiply_add_fusion.1
  920.3 6.3 copy.47
  926.6 4.2 slice.12
  (46 shorter events, 38.9 us)
Async XLA Ops:
  7.2 205.5 %reduce-scatter.2.cloned.1.call-start = ((), (), s32[]{:S(2)}) async-start(), calls=%async_computation.7 | async-start | bytes 35389440 | tf_op jit(solution)/shard_map/reduce_scatter | solution.py:44
  7.2 2.0 copy-start.2
  11.4 5.8 copy-start.3
  11.4 83.9 %all-to-all-start = ((bf16[8,7,128,256]{3,2,1,0:T(8,128)(2,1)}), bf16[8,7,128,256]{3,2,1,0:T(8,128)(2,1)}, u32[]{:S(2)}, u32[]{:S(2)}) async-start(bf16[8,7,128,256]{3,2,1,0:T(8,128)(2,1)} %bitcast.45), calls=%async_computation.1 | async-start | bytes 7340032 | tf_op jit(solution)/shard_map/all_to_all | solution.py:33
  95.4 85.3 %all-to-all-start.1 = ((bf16[8,7,128,256]{3,2,1,0:T(8,128)(2,1)}), bf16[8,7,128,256]{3,2,1,0:T(8,128)(2,1)}, u32[]{:S(2)}, u32[]{:S(2)}) async-start(bf16[8,7,128,256]{3,2,1,0:T(8,128)(2,1)} %bitcast.44), calls=%async_computation.2 | async-start | bytes 7340032 | tf_op jit(solution)/shard_map/all_to_all | solution.py:33
  103.1 650.7 %all-gather.4.cloned.1.call-start = ((), (), s32[]{:S(2)}) async-start(), calls=%async_computation.8 | async-start | bytes 18350080 | tf_op jit(solution)/shard_map/all_gather | solution.py:68
  312.2 98.5 %collective-permute-start = (bf16[7,1024,256]{2,1,0:T(8,128)(2,1)}, bf16[7,1024,256]{2,1,0:T(8,128)(2,1)}, u32[]{:S(2)}, u32[]{:S(2)}) collective-permute-start(bf16[7,1024,256]{2,1,0:T(8,128)(2,1)} %bitcast.9), channel_id=1, source_target_pairs={{0,1},{1,2},{2,3},{3,0},{4,5},{5,6},{6,7},{7,4},{8,9},{9,10},{10,1... | collective-permute-start | bytes 11010056 | tf_op jit(solution)/shard_map/ppermute | solution.py:55
  410.7 61.3 %collective-permute-start.1 = (bf16[7,1024,256]{2,1,0:T(8,128)(2,1)}, bf16[7,1024,256]{2,1,0:T(8,128)(2,1)}, u32[]{:S(2)}, u32[]{:S(2)}) collective-permute-start(bf16[7,1024,256]{2,1,0:T(8,128)(2,1)} %collective-permute-done), channel_id=1, source_target_pairs={{0,1},{1,2},{2,3},{3,0},{4,5},{5,6},{6,7},{7,4},{8,9},{9,10},{10,1... | collective-permute-start | bytes 11010056 | tf_op jit(solution)/shard_map/ppermute | solution.py:55
  472.0 42.6 %collective-permute-start.2 = (bf16[7,1024,256]{2,1,0:T(8,128)(2,1)}, bf16[7,1024,256]{2,1,0:T(8,128)(2,1)}, u32[]{:S(2)}, u32[]{:S(2)}) collective-permute-start(bf16[7,1024,256]{2,1,0:T(8,128)(2,1)} %collective-permute-done.1), channel_id=1, source_target_pairs={{0,1},{1,2},{2,3},{3,0},{4,5},{5,6},{6,7},{7,4},{8,9},{9,10},{10,1... | collective-permute-start | bytes 11010056 | tf_op jit(solution)/shard_map/ppermute | solution.py:55
  535.1 9.7 %copy-start.1 = (bf16[7,1024,2048]{2,1,0:T(8,128)(2,1)}, bf16[7,1024,2048]{2,1,0:T(8,128)(2,1)S(1)}, u32[]{:S(2)}) copy-start(bf16[7,1024,2048]{2,1,0:T(8,128)(2,1)S(1)} %constant_dynamic-update-slice_fusion) | copy-start | bytes 88080384
  562.0 82.8 %all-to-all-start.5 = ((bf16[8,7,128,256]{3,2,1,0:T(8,128)(2,1)}), bf16[8,7,128,256]{3,2,1,0:T(8,128)(2,1)}, u32[]{:S(2)}, u32[]{:S(2)}) async-start(bf16[8,7,128,256]{3,2,1,0:T(8,128)(2,1)} %bitcast.48), calls=%async_computation.6 | async-start | bytes 7340032 | tf_op jit(solution)/shard_map/all_to_all | solution.py:37
  644.9 140.2 %all-to-all-start.4 = ((bf16[8,7,128,256]{2,3,1,0:T(8,128)(2,1)}), bf16[8,7,128,256]{2,3,1,0:T(8,128)(2,1)}, u32[]{:S(2)}, u32[]{:S(2)}) async-start(bf16[8,7,128,256]{2,3,1,0:T(8,128)(2,1)} %copy.48), calls=%async_computation.5 | async-start | bytes 7340032 | tf_op jit(solution)/shard_map/all_to_all | solution.py:37
  782.7 8.6 copy-start.4
  782.7 117.4 %copy-start.5 = (f32[2,2048]{1,0:T(2,128)S(1)}, f32[2,2048]{1,0:T(2,128)}, u32[]{:S(2)}) copy-start(f32[2,2048]{1,0:T(2,128)} %param.15) | copy-start | bytes 49156
  785.0 135.2 %all-to-all-start.3 = ((bf16[8,7,128,256]{2,3,1,0:T(8,128)(2,1)}), bf16[8,7,128,256]{2,3,1,0:T(8,128)(2,1)}, u32[]{:S(2)}, u32[]{:S(2)}) async-start(bf16[8,7,128,256]{2,3,1,0:T(8,128)(2,1)} %copy.46), calls=%async_computation.4 | async-start | bytes 7340032 | tf_op jit(solution)/shard_map/all_to_all | solution.py:37
  900.8 15.1 %slice-start = ((s8[7077888]{0:T(1024)(128)(4,1)}), s8[2883584]{0:T(1024)(128)(4,1)S(1)}, s32[]{:S(2)}) async-start(s8[7077888]{0:T(1024)(128)(4,1)} %bitcast.53), calls=%async_computation.9 | async-start | bytes 5767168
  907.1 8.8 copy-start
  907.1 8.8 slice-start.1
Sparse Core Ops, SparseCore 0:
  10.6 201.9 reduce-scatter.1
  314.0 133.9 all-gather.3
